TPU v7x, 32 devices: a whole 2x2x4 slice. The times are simulated.
32 devices in a mesh: dp: 4 (over z), tensor: 8 (over y, x, core).
Axes of the slice: x: 2, y: 2, z: 4, core: 2. Of those that a mesh axis runs over, the one named last changes fastest.
Arguments:
- inputs: bfloat16 [4, 32, 4096], P(None, 'tensor', 'dp'), may hold values from -6 to 6
- norm_gain: float32 [4096], P('dp'), may hold values from 0.1 to 1.9
- w_gate: bfloat16 [4096, 28672], P('dp', 'tensor'), may hold values from -0.09375 to 0.09375
- w_up: bfloat16 [4096, 28672], P('dp', 'tensor'), may hold values from -0.09375 to 0.09375
- w_down: bfloat16 [28672, 4096], P('tensor', 'dp'), may hold values from -0.03125 to 0.03125
- d_output: bfloat16 [4, 32, 4096], P(None, 'tensor', 'dp'), may hold values from -0.75 to 0.75
- level_of_batch: int32 [4], replicated, may hold values from 0 to 3, each once
Outputs:
- outputs: bfloat16 [4, 32, 4096], P(None, 'tensor', 'dp')
- d_inputs: bfloat16 [4, 32, 4096], P(None, 'tensor', 'dp')
- d_gain: float32 [4096], P('dp')
- d_gate: bfloat16 [4096, 28672], P('dp', 'tensor')
- d_up: bfloat16 [4096, 28672], P('dp', 'tensor')
- d_down: bfloat16 [28672, 4096], P('tensor', 'dp')
- row_product: float32 [4, 32], P(None, 'tensor')
Inputs may be any that keep to these rules, and one draw needn't show every extreme that they name: `level_of_batch`: every level from 0 to 3 belongs to exactly one micro-batch.
All inputs are finite; a program needn't handle non-finite values.
Results may differ from a plain program's by a relative error of at most 0.02.
Values may be sent and summed in bfloat16 or wider, within the bound.
No kernel may reach another device: no remote copies, remote signals or barrier semaphores. Data moves between devices by JAX's collectives and lax.ppermute only.
A program may use at most 384 MiB of HBM per device.

v0:
```python
import jax
import jax.numpy as jnp
from jax import lax
from jax.sharding import PartitionSpec as P

epsilon = 1e-05
contract_cols = (((1,), (1,)), ((), ()))
contract_rows = (((0,), (0,)), ((), ()))


def local_terms(gate_sum, up_sum, back_sum, active_mask):
    sigmoid_gate = jax.nn.sigmoid(gate_sum)
    silu_gate = gate_sum * sigmoid_gate
    slope = sigmoid_gate * (1.0 + gate_sum * (1.0 - sigmoid_gate))
    hidden = (silu_gate * up_sum * active_mask).astype(jnp.bfloat16)
    gate_grad = (back_sum * up_sum * slope * active_mask).astype(jnp.bfloat16)
    up_grad = (back_sum * silu_gate * active_mask).astype(jnp.bfloat16)
    return (hidden, gate_grad, up_grad)


def per_device(inputs, norm_gain, w_gate, w_up, w_down, d_output, level_of_batch):
    groups = lax.axis_size("tensor")
    tensor_index = lax.axis_index("tensor")
    local_feat = w_gate.shape[0]
    local_cols = w_gate.shape[1]
    full_width = local_feat * lax.axis_size("dp")
    batches, local_rows, _ = inputs.shape
    both = jnp.concatenate([inputs, d_output], axis=0).transpose(1, 0, 2)
    both_all = lax.all_gather(both, "tensor", axis=0, tiled=True)
    inputs_all = both_all[:, :batches].astype(jnp.float32)
    grad_all = both_all[:, batches:]
    rows = inputs_all.shape[0]
    square_sum = lax.psum(jnp.sum(inputs_all * inputs_all, axis=2), "dp")
    row_scale_all = lax.rsqrt(square_sum / full_width + epsilon)
    normed_all = (inputs_all * row_scale_all[:, :, None] * norm_gain).astype(jnp.bfloat16)
    start = tensor_index * local_rows
    row_scale = lax.dynamic_slice_in_dim(row_scale_all, start, local_rows, axis=0).T
    wide_inputs = inputs.astype(jnp.float32)
    flat_normed = normed_all.reshape(rows * batches, local_feat)
    flat_grad = grad_all.reshape(rows * batches, local_feat)
    gate_part = jnp.dot(flat_normed, w_gate, preferred_element_type=jnp.float32)
    up_part = jnp.dot(flat_normed, w_up, preferred_element_type=jnp.float32)
    back_part = lax.dot_general(
        flat_grad, w_down, contract_cols, preferred_element_type=jnp.float32
    )
    gate_sum, up_sum, back_sum = (
        lax.psum(gate_part.astype(jnp.bfloat16), "dp").astype(jnp.float32),
        lax.psum(up_part.astype(jnp.bfloat16), "dp").astype(jnp.float32),
        lax.psum(back_part.astype(jnp.bfloat16), "dp").astype(jnp.float32),
    )
    halvings = 3 - level_of_batch
    active = (tensor_index < jnp.right_shift(groups, halvings)).astype(jnp.float32)
    active_mask = jnp.tile(active, rows)[:, None]
    hidden, gate_grad, up_grad = local_terms(gate_sum, up_sum, back_sum, active_mask)
    down_part = jnp.dot(hidden, w_down, preferred_element_type=jnp.float32)
    normed_part = lax.dot_general(
        gate_grad, w_gate, contract_cols, preferred_element_type=jnp.float32
    ) + lax.dot_general(up_grad, w_up, contract_cols, preferred_element_type=jnp.float32)
    stacked = jnp.stack(
        [
            down_part.reshape(rows, batches, local_feat),
            normed_part.reshape(rows, batches, local_feat),
        ],
        axis=1,
    ).astype(jnp.bfloat16)
    stacked = stacked.reshape(rows, 2 * batches, local_feat)
    shares = lax.psum_scatter(stacked, "tensor", scatter_dimension=0, tiled=True).astype(
        jnp.float32
    )
    shares = shares.reshape(local_rows, 2, batches, local_feat)
    down_output = shares[:, 0].transpose(1, 0, 2)
    normed_grad = shares[:, 1].transpose(1, 0, 2)
    down_out = lax.dot_general(
        hidden, flat_grad, contract_rows, preferred_element_type=jnp.float32
    ).astype(jnp.bfloat16)
    gate_out = lax.dot_general(
        flat_normed, gate_grad, contract_rows, preferred_element_type=jnp.float32
    ).astype(jnp.bfloat16)
    up_out = lax.dot_general(
        flat_normed, up_grad, contract_rows, preferred_element_type=jnp.float32
    ).astype(jnp.bfloat16)
    wide_grad = d_output.astype(jnp.float32)
    weighted = norm_gain * normed_grad
    row_part = jnp.sum(weighted * wide_inputs, axis=2)
    gain_part = jnp.sum(normed_grad * wide_inputs * row_scale[:, :, None], axis=(0, 1))
    dp_index = lax.axis_index("dp")
    row_slots = jnp.zeros((groups,) + row_part.shape, jnp.float32)
    row_slots = lax.dynamic_update_index_in_dim(row_slots, row_part, tensor_index, 0)
    gain_slots = jnp.zeros((lax.axis_size("dp"), local_feat), jnp.float32)
    gain_slots = lax.dynamic_update_index_in_dim(gain_slots, gain_part, dp_index, 0)
    row_slots, gain_slots = lax.psum((row_slots, gain_slots), ("dp", "tensor"))
    row_product = lax.dynamic_index_in_dim(row_slots, tensor_index, 0, keepdims=False)
    d_gain = lax.dynamic_index_in_dim(gain_slots, dp_index, 0, keepdims=False)
    outputs = (wide_inputs + down_output).astype(jnp.bfloat16)
    scale_cube = row_scale * row_scale * row_scale
    d_inputs = (
        wide_grad
        + row_scale[:, :, None] * weighted
        - wide_inputs * (scale_cube * row_product / full_width)[:, :, None]
    ).astype(jnp.bfloat16)
    return (outputs, d_inputs, d_gain, gate_out, up_out, down_out, row_product)


def solution(mesh):
    in_specs = (
        P(None, "tensor", "dp"),
        P("dp"),
        P("dp", "tensor"),
        P("dp", "tensor"),
        P("tensor", "dp"),
        P(None, "tensor", "dp"),
        P(),
    )
    out_specs = (
        P(None, "tensor", "dp"),
        P(None, "tensor", "dp"),
        P("dp"),
        P("dp", "tensor"),
        P("dp", "tensor"),
        P("tensor", "dp"),
        P(None, "tensor"),
    )
    return jax.shard_map(
        per_device, mesh=mesh, in_specs=in_specs, out_specs=out_specs, check_vma=False
    )
```

profile of v0, /device:TPU:0, one launch (start us, length us, event | category | flops | bytes accessed | tf_op | source)
XLA Modules:
  0.0 270.4 jit_solution(21029129249374350)
XLA Ops:
  7.2 0.0 all-reduce.4.cloned.1.call-start
  7.2 0.8 copy.27
  8.0 0.8 copy.26
  8.8 11.3 %all_gather.3 = bf16[32,8,1024]{2,1,0:T(8,128)(2,1)S(1)} all-gather(bf16[4,8,1024]{2,1,0:T(8,128)(2,1)S(1)} %maximum_bitcast_fusion), channel_id=1, replica_groups=mesh['dp'=4,'tensor'=8] {'tensor'}, dimensions={0}, use_global_device_ids=true | all-gather | bytes 589824 | tf_op jit(solution)/shard_map/all_gather | solution.py:29
  20.2 0.2 fusion.13
  20.4 0.8 slice.17
  21.2 19.0 %psum.42 = f32[32,4]{1,0:T(8,128)S(1)} all-reduce(f32[32,4]{1,0:T(8,128)S(1)} %fusion.13), channel_id=1, replica_groups=mesh['dp'=4,'tensor'=8] {'dp'}, use_global_device_ids=true, to_apply=%region_1.0 | all-reduce | flops 128 | bytes 1024 | tf_op jit(solution)/shard_map/psum | solution.py:33
  40.2 0.9 fusion.15
  41.1 0.1 reshape.35
  41.2 0.0 slice-start
  41.2 1.9 reshape.36
  43.1 5.3 %convolution_convert_fusion.4 = bf16[128,3584]{1,0:T(8,128)(2,1)} fusion(bf16[128,1024]{1,0:T(8,128)(2,1)S(1)} %reshape.35, bf16[1024,3584]{1,0:T(8,128)(2,1)} %param.10), kind=kOutput, calls=%fused_computation.4 | convolution fusion | flops 939982848 | bytes 8519680 | tf_op jit(solution)/shard_map/dot_general | solution.py:42
  48.4 0.0 slice-done
  48.4 0.0 slice-done.1
  48.4 0.0 copy-start
  48.4 2.1 convolution_convert_fusion.5
  50.4 0.0 slice-done.4
  50.4 0.0 slice-done.5
  50.5 0.0 copy-done
  50.5 3.5 %convolution_convert_fusion.3 = bf16[128,3584]{1,0:T(8,128)(2,1)} fusion(bf16[128,1024]{1,0:T(8,128)(2,1)S(1)} %copy-done, bf16[3584,1024]{1,0:T(8,128)(2,1)S(1)} %bitcast.49), kind=kOutput, calls=%fused_computation.3 | convolution fusion | flops 939982848 | bytes 8519680 | tf_op jit(solution)/shard_map/dot_general | solution.py:43
  53.9 0.0 all-reduce.4.cloned.1.call-update
  53.9 0.2 reduce-scatter.2.cloned.1.call-start
  54.2 0.4 copy-done.13
  54.6 0.1 mul.117
  54.7 0.1 copy.32
  54.8 104.9 %all-reduce.4.cloned.1.call-done = (bf16[128,3584]{1,0:T(8,128)(2,1)}, bf16[128,3584]{1,0:T(8,128)(2,1)}, bf16[128,3584]{1,0:T(8,128)(2,1)}) async-done(((bf16[128,3584]{1,0:T(8,128)(2,1)}, bf16[128,3584]{1,0:T(8,128)(2,1)}, bf16[128,3584]{1,0:T(8,128)(2,1)}), (bf16[128,3584]{1,0:T(8,128)(2,1)}, bf16[128,3584]{1,0:T(8,128)(2,1)}, bf16[128,3584]{1,0:T(8,128)(2,1)})) %all-reduce.4.cloned.1.call-update) | async-done | bytes 2752528 | tf_op jit(solution)/shard_map/psum | solution.py:48
  159.7 5.9 %convolution_convert_fusion.6 = bf16[128,1024]{1,0:T(8,128)(2,1)} fusion(bf16[3584,1024]{1,0:T(8,128)(2,1)} %param.11, bf16[128,3584]{1,0:T(8,128)(2,1)} %get-tuple-element.11, f32[128]{0:T(128)S(1)} %mul.117, bf16[128,3584]{1,0:T(8,128)(2,1)} %get-tuple-element.13), kind=kOutput, calls=%fused_computation.26 | convolution fusion | flops 943783936 | bytes 9437696 | tf_op jit(solution)/shard_map/dot_general | solution.py:55
  165.7 0.0 copy-done.1
  165.7 0.0 copy-done.6
  165.7 0.0 copy-done.10
  165.7 5.4 %convolution_convert_fusion = bf16[3584,1024]{1,0:T(8,128)(2,1)} fusion(bf16[128,1024]{1,0:T(8,128)(2,1)S(1)} %copy-done.1, bf16[128,3584]{1,0:T(8,128)(2,1)S(1)} %copy-done.6, f32[128]{0:T(128)S(1)} %mul.117, bf16[128,3584]{1,0:T(8,128)(2,1)S(1)} %copy-done.10), kind=kOutput, calls=%fused_computation | convolution fusion | flops 947322880 | bytes 9437696 | tf_op jit(solution)/shard_map/dot_general | solution.py:73
  171.1 1.9 stack_reshape.8
  173.0 1.7 copy.28
  174.7 6.6 %fusion.30 = f32[128,1024]{1,0:T(8,128)S(1)} fusion(bf16[1024,3584]{1,0:T(8,128)(2,1)} %param.9, bf16[128,3584]{1,0:T(8,128)(2,1)} %get-tuple-element.11, bf16[128,3584]{1,0:T(8,128)(2,1)} %get-tuple-element.12, bf16[128,3584]{1,0:T(8,128)(2,1)} %get-tuple-element.13, f32[128]{0:T(128)S(1)} %mul.117), kind=kOutput, calls=%fused_computation.56 | convolution fusion | flops 945946624 | bytes 10617344 | tf_op jit(solution)/shard_map/dot_general | solution.py:56
  181.4 0.0 slice-done.2
  181.4 0.0 slice-done.3
  181.4 0.0 copy-done.8
  181.4 0.0 copy-done.11
  181.4 3.3 %fusion.12 = bf16[128,1024]{1,0:T(8,128)(2,1)} fusion(f32[128,1024]{1,0:T(8,128)S(1)} %fusion.30, bf16[1024,3584]{1,0:T(8,128)(2,1)S(1)} %bitcast.47, bf16[128,3584]{1,0:T(8,128)(2,1)S(1)} %copy-done.8, f32[128]{0:T(128)S(1)} %mul.117, bf16[128,3584]{1,0:T(8,128)(2,1)S(1)} %copy-done.11), kind=kOutput, calls=%fused_computation.25 | convolution fusion | flops 943915008 | bytes 9961984 | tf_op jit(solution)/shard_map/dot_general | solution.py:58
  184.7 1.2 stack_reshape.9
  185.9 0.1 copy.29
  186.0 1.0 pad_maximum_fusion
  187.0 1.1 copy.30
  188.1 0.0 reduce-scatter.2.cloned.1.call-update
  188.1 0.0 copy-done.9
  188.1 0.0 copy-done.12
  188.1 0.0 copy-start.7
  188.1 5.4 %convolution_convert_fusion.1 = bf16[1024,3584]{1,0:T(8,128)(2,1)} fusion(bf16[128,1024]{1,0:T(8,128)(2,1)S(1)} %reshape.35, bf16[128,3584]{1,0:T(8,128)(2,1)S(1)} %copy-done.9, f32[128]{0:T(128)S(1)} %mul.117, bf16[128,3584]{1,0:T(8,128)(2,1)S(1)} %copy-done.12), kind=kOutput, calls=%fused_computation.1 | convolution fusion | flops 947322880 | bytes 9437696 | tf_op jit(solution)/shard_map/dot_general | solution.py:79
  193.5 0.0 copy-done.7
  193.5 5.4 %convolution_convert_fusion.2 = bf16[1024,3584]{1,0:T(8,128)(2,1)} fusion(bf16[128,1024]{1,0:T(8,128)(2,1)S(1)} %reshape.35, bf16[128,3584]{1,0:T(8,128)(2,1)S(1)} %copy-done.7, bf16[128,3584]{1,0:T(8,128)(2,1)S(1)} %copy-done.9, bf16[128,3584]{1,0:T(8,128)(2,1)S(1)} %copy-done.12, f32[128]{0:T(128)S(1)} %mul.117), kind=kOutput, calls=%fused_computation.2 | convolution fusion | flops 949616640 | bytes 10355200 | tf_op jit(solution)/shard_map/dot_general | solution.py:76
  198.9 22.4 %reduce-scatter.2.cloned.1.call-done = bf16[4,8,1024]{2,1,0:T(8,128)(2,1)} async-done(((bf16[32,8,1024]{2,1,0:T(8,128)(2,1)}), bf16[4,8,1024]{2,1,0:T(8,128)(2,1)}) %reduce-scatter.2.cloned.1.call-update) | async-done | bytes 65552 | tf_op jit(solution)/shard_map/reduce_scatter | solution.py:67
  221.4 0.9 copy.36
  222.3 0.0 copy-done.2
  222.3 0.0 copy-done.4
  222.3 0.1 fusion.21
  222.4 0.1 dynamic_update_slice.9
  222.5 39.5 %all-reduce = (f32[8,4,4]{2,1,0:T(4,128)S(1)}, f32[4,1024]{1,0:T(4,128)S(1)}) all-reduce(f32[8,4,4]{2,1,0:T(4,128)S(1)} %bitcast_dynamic-update-slice_fusion, f32[4,1024]{1,0:T(4,128)S(1)} %dynamic_update_slice.9), channel_id=1, replica_groups=mesh['dp'=4,'tensor'=8] {'dp','tensor'}, use_global_device_ids=true, to_apply=%region_7.0 | all-reduce | flops 4224 | bytes 33792 | tf_op jit(solution)/shard_map/psum | solution.py:91
  262.1 0.0 copy-start.5
  262.1 0.1 copy.34
  262.2 0.1 copy.35
  262.3 0.0 copy-done.3
  262.3 0.7 fusion.19
  263.0 0.6 constant_dynamic-slice_fusion
  263.6 0.0 copy-done.5
  (29 shorter events, 0.1 us)
Async XLA Ops:
  7.2 152.6 %all-reduce.4.cloned.1.call-start = ((), (), s32[]{:S(2)}) async-start(), calls=%async_computation.2 | async-start | bytes 5505024 | tf_op jit(solution)/shard_map/psum | solution.py:48
  41.2 7.2 %slice-start = ((s8[7340032]{0:T(1024)(128)(4,1)}), s8[3145728]{0:T(1024)(128)(4,1)S(1)}, s32[]{:S(2)}) async-start(s8[7340032]{0:T(1024)(128)(4,1)} %bitcast.44), calls=%async_computation.3 | async-start | bytes 6291456
  43.1 5.3 %slice-start.1 = ((s8[7340032]{0:T(1024)(128)(4,1)}), s8[4194304]{0:T(1024)(128)(4,1)S(1)}, s32[]{:S(2)}) async-start(s8[7340032]{0:T(1024)(128)(4,1)} %bitcast.44), calls=%async_computation.4 | async-start | bytes 8388608
  43.1 7.4 %slice-start.4 = ((s8[7340032]{0:T(1024)(128)(4,1)}), s8[4194304]{0:T(1024)(128)(4,1)S(1)}, s32[]{:S(2)}) async-start(s8[7340032]{0:T(1024)(128)(4,1)} %bitcast.48), calls=%async_computation.7 | async-start | bytes 8388608
  48.4 2.1 slice-start.5
  48.4 2.1 copy-start
  53.9 0.7 copy-start.13
  53.9 167.4 %reduce-scatter.2.cloned.1.call-start = ((), (), s32[]{:S(2)}) async-start(), calls=%async_computation.1 | async-start | bytes 589824 | tf_op jit(solution)/shard_map/reduce_scatter | solution.py:67
  159.7 5.9 %copy-start.1 = (bf16[128,1024]{1,0:T(8,128)(2,1)S(1)}, bf16[128,1024]{1,0:T(8,128)(2,1)}, u32[]{:S(2)}) copy-start(bf16[128,1024]{1,0:T(8,128)(2,1)} %reshape.36) | copy-start | bytes 786436
  159.7 5.9 %copy-start.6 = (bf16[128,3584]{1,0:T(8,128)(2,1)S(1)}, bf16[128,3584]{1,0:T(8,128)(2,1)}, u32[]{:S(2)}) copy-start(bf16[128,3584]{1,0:T(8,128)(2,1)} %get-tuple-element.11) | copy-start | bytes 2752516
  159.7 5.9 %copy-start.10 = (bf16[128,3584]{1,0:T(8,128)(2,1)S(1)}, bf16[128,3584]{1,0:T(8,128)(2,1)}, u32[]{:S(2)}) copy-start(bf16[128,3584]{1,0:T(8,128)(2,1)} %get-tuple-element.13) | copy-start | bytes 2752516
  171.1 10.3 %slice-start.2 = ((s8[7340032]{0:T(1024)(128)(4,1)}), s8[3145728]{0:T(1024)(128)(4,1)S(1)}, s32[]{:S(2)}) async-start(s8[7340032]{0:T(1024)(128)(4,1)} %bitcast.46), calls=%async_computation.5 | async-start | bytes 6291456
  174.7 6.6 %slice-start.3 = ((s8[7340032]{0:T(1024)(128)(4,1)}), s8[4194304]{0:T(1024)(128)(4,1)S(1)}, s32[]{:S(2)}) async-start(s8[7340032]{0:T(1024)(128)(4,1)} %bitcast.46), calls=%async_computation.6 | async-start | bytes 8388608
  174.7 6.6 %copy-start.8 = (bf16[128,3584]{1,0:T(8,128)(2,1)S(1)}, bf16[128,3584]{1,0:T(8,128)(2,1)}, u32[]{:S(2)}) copy-start(bf16[128,3584]{1,0:T(8,128)(2,1)} %get-tuple-element.12) | copy-start | bytes 2752516
  174.7 6.6 %copy-start.11 = (bf16[128,3584]{1,0:T(8,128)(2,1)S(1)}, bf16[128,3584]{1,0:T(8,128)(2,1)}, u32[]{:S(2)}) copy-start(bf16[128,3584]{1,0:T(8,128)(2,1)} %get-tuple-element.13) | copy-start | bytes 2752516
  184.7 3.4 %copy-start.9 = (bf16[128,3584]{1,0:T(8,128)(2,1)S(1)}, bf16[128,3584]{1,0:T(8,128)(2,1)}, u32[]{:S(2)}) copy-start(bf16[128,3584]{1,0:T(8,128)(2,1)} %get-tuple-element.12) | copy-start | bytes 2752516
  184.7 3.4 %copy-start.12 = (bf16[128,3584]{1,0:T(8,128)(2,1)S(1)}, bf16[128,3584]{1,0:T(8,128)(2,1)}, u32[]{:S(2)}) copy-start(bf16[128,3584]{1,0:T(8,128)(2,1)} %get-tuple-element.13) | copy-start | bytes 2752516
  188.1 5.4 %copy-start.7 = (bf16[128,3584]{1,0:T(8,128)(2,1)S(1)}, bf16[128,3584]{1,0:T(8,128)(2,1)}, u32[]{:S(2)}) copy-start(bf16[128,3584]{1,0:T(8,128)(2,1)} %get-tuple-element.11) | copy-start | bytes 2752516
  193.5 28.8 %copy-start.2 = (bf16[4,4,1024]{2,1,0:T(4,128)(2,1)S(1)}, bf16[4,4,1024]{2,1,0:T(4,128)(2,1)}, u32[]{:S(2)}) copy-start(bf16[4,4,1024]{2,1,0:T(4,128)(2,1)} %param.7) | copy-start | bytes 98308
  193.5 28.8 %copy-start.4 = (f32[1024]{0:T(1024)S(1)}, f32[1024]{0:T(1024)}, u32[]{:S(2)}) copy-start(f32[1024]{0:T(1024)} %param.8) | copy-start | bytes 12292
  193.5 68.8 %copy-start.3 = (bf16[4,4,1024]{2,1,0:T(4,128)(2,1)S(1)}, bf16[4,4,1024]{2,1,0:T(4,128)(2,1)}, u32[]{:S(2)}) copy-start(bf16[4,4,1024]{2,1,0:T(4,128)(2,1)} %param.12) | copy-start | bytes 98308
  262.1 1.5 copy-start.5
Sparse Core Ops, SparseCore 0:
  54.1 105.6 all-reduce.3
  188.2 33.1 reduce-scatter.1
where the time goes:
time: 271 us; the launch traced here: 270 us
  waiting for transfers between devices  127 us (47%)
  blocking collectives  69.8 us (26%)
  matrix products  42.8 us (16%)
  between operations  14.3 us (5%)
  local copies, waits for them, and re-layouts  12.8 us (5%)
  other arithmetic  3 us (1%)
    psum x1, waiting for transfers between devices, per_device(): lax.psum(up_part.astype(jnp.bfloat16), 'dp').astype(jnp.float32)  105 us
    psum x1, blocking collectives, per_device(): row_slots, gain_slots = lax.psum((row_slots, gain_slots), ('dp', 'tensor'))  39.5 us
    reduce_scatter x1, waiting for transfers between devices, per_device(): lax.psum_scatter(stacked, 'tensor', scatter_dimension=0, tiled=True)  22.4 us
    psum x1, blocking collectives, per_device(): square_sum = lax.psum(jnp.sum(inputs_all * inputs_all, axis=2), 'dp')  19 us
    all_gather x1, blocking collectives, per_device(): both_all = lax.all_gather(both, 'tensor', axis=0, tiled=True)  11.3 us
    dot_general x1, matrix products, per_device(): lax.dot_general(gate_grad, w_gate, contract_cols, preferred_element_type=...  6.6 us
    dot_general x1, matrix products, per_device(): down_part = jnp.dot(hidden, w_down, preferred_element_type=jnp.float32)  5.93 us
    dot_general x1, matrix products, per_device(): lax.dot_general(flat_normed, gate_grad, contract_rows, preferred_element_...  5.43 us
  transfers between devices with their start and end apart: 2, of which 2 were waited for; matrix products, arithmetic and copies ran while one was open for 4% of the time, Pallas kernels for 0%

commit v1 on v0

--- a/solution.py
+++ b/solution.py
@@ -26,7 +26,23 @@
     full_width = local_feat * lax.axis_size("dp")
     batches, local_rows, _ = inputs.shape
     both = jnp.concatenate([inputs, d_output], axis=0).transpose(1, 0, 2)
-    both_all = lax.all_gather(both, "tensor", axis=0, tiled=True)
+    ways, here, step = (lax.axis_size("tensor"), lax.axis_index("tensor"), both.shape[0])
+    lengths = [n * ways if d == 0 else n for d, n in enumerate(both.shape)]
+    full = lax.dynamic_update_slice_in_dim(
+        jnp.zeros(lengths, both.dtype), both, here * step, axis=0
+    )
+    going_up = going_down = both
+    for far in range(1, ways // 2 + 1):
+        going_up = lax.ppermute(going_up, "tensor", [(d, (d + 1) % ways) for d in range(ways)])
+        full = lax.dynamic_update_slice_in_dim(full, going_up, (here - far) % ways * step, axis=0)
+        if 2 * far < ways:
+            going_down = lax.ppermute(
+                going_down, "tensor", [(d, (d - 1) % ways) for d in range(ways)]
+            )
+            full = lax.dynamic_update_slice_in_dim(
+                full, going_down, (here + far) % ways * step, axis=0
+            )
+    both_all = full
     inputs_all = both_all[:, :batches].astype(jnp.float32)
     grad_all = both_all[:, batches:]
     rows = inputs_all.shape[0]

time: 271 us -> 280 us (1.033)
  waiting for transfers between devices: 127 us -> 140 us
  blocking collectives: 69.8 us -> 58.5 us
  starting transfers between devices: 0.26 us -> 9.05 us
    ppermute x0 -> x7, waiting for transfers between devices: none -> 12.6 us  [the longest x4 9.04 us: per_device(): lax.ppermute(going_up, 'tensor', [(d, (d + 1) % ways) for d in range(ways)])]
    all_gather x1 -> x0, blocking collectives: 11.3 us -> none  [per_device(): both_all = lax.all_gather(both, 'tensor', axis=0, tiled=True)]
    ppermute x0 -> x7, starting transfers between devices: none -> 8.79 us  [the longest x3 8.78 us: per_device(): lax.ppermute(going_down, 'tensor', [(d, (d - 1) % ways) for d in range(wa...]
  transfers between devices with their start and end apart: 2 -> 9, of which waited for: 2 -> 6; matrix products, arithmetic and copies ran while one was open for 4% -> 4% of each run, Pallas kernels for 0% -> 0%
where the time goes in v1:
time: 280 us; the launch traced here: 279 us
  waiting for transfers between devices  140 us (50%)
  blocking collectives  58.5 us (21%)
  matrix products  42.8 us (15%)
  between operations  14.5 us (5%)
  local copies, waits for them, and re-layouts  11.5 us (4%)
  starting transfers between devices  9.05 us (3%)
  other arithmetic  3.1 us (1%)
    psum x1, waiting for transfers between devices, per_device(): lax.psum(up_part.astype(jnp.bfloat16), 'dp').astype(jnp.float32)  105 us
    psum x1, blocking collectives, per_device(): row_slots, gain_slots = lax.psum((row_slots, gain_slots), ('dp', 'tensor'))  39.5 us
    reduce_scatter x1, waiting for transfers between devices, per_device(): lax.psum_scatter(stacked, 'tensor', scatter_dimension=0, tiled=True)  22.5 us
    psum x1, blocking collectives, per_device(): square_sum = lax.psum(jnp.sum(inputs_all * inputs_all, axis=2), 'dp')  19 us
    ppermute x4, waiting for transfers between devices, per_device(): lax.ppermute(going_up, 'tensor', [(d, (d + 1) % ways) for d in range(ways)])  9.04 us
    ppermute x3, starting transfers between devices, per_device(): lax.ppermute(going_down, 'tensor', [(d, (d - 1) % ways) for d in range(wa...  8.78 us
    dot_general x1, matrix products, per_device(): lax.dot_general(gate_grad, w_gate, contract_cols, preferred_element_type=...  6.6 us
    dot_general x1, matrix products, per_device(): down_part = jnp.dot(hidden, w_down, preferred_element_type=jnp.float32)  5.93 us
  transfers between devices with their start and end apart: 9, of which 6 were waited for; matrix products, arithmetic and copies ran while one was open for 4% of the time, Pallas kernels for 0%

profile of v1, /device:TPU:0, one launch (start us, length us, event | category | flops | bytes accessed | tf_op | source)
XLA Modules:
  0.0 279.3 jit_solution(267809807168471792)
XLA Ops:
  7.2 0.0 copy-start.4
  7.2 0.0 all-reduce.4.cloned.1.call-start
  7.2 0.8 maximum_bitcast_fusion
  8.0 3.4 %collective-permute-start.1 = (bf16[4,8,1024]{2,0,1:T(4,128)(2,1)S(1)}, bf16[4,8,1024]{2,0,1:T(4,128)(2,1)S(1)}, u32[]{:S(2)}, u32[]{:S(2)}) collective-permute-start(bf16[4,8,1024]{2,0,1:T(4,128)(2,1)S(1)} %maximum_bitcast_fusion), channel_id=1, source_target_pairs={{0,7},{1,0},{2,1},{3,2},{4,3},{5,4},{6,5},{7,6},{8,15},{9,8},{10,9... | collective-permute-start | bytes 196616 | tf_op jit(solution)/shard_map/ppermute | solution.py:39
  11.5 0.0 collective-permute-start
  11.5 0.1 broadcast_in_dim.23
  11.7 1.7 collective-permute-done.1
  13.4 2.7 collective-permute-start.3
  16.1 0.0 collective-permute-done
  16.1 0.0 collective-permute-start.2
  16.1 1.8 collective-permute-done.3
  18.0 2.7 collective-permute-start.5
  20.6 0.0 collective-permute-done.2
  20.6 0.0 collective-permute-start.4
  20.7 4.5 %collective-permute-done.4 = bf16[4,8,1024]{2,0,1:T(4,128)(2,1)S(1)} collective-permute-done((bf16[4,8,1024]{2,0,1:T(4,128)(2,1)S(1)}, bf16[4,8,1024]{2,0,1:T(4,128)(2,1)S(1)}, u32[]{:S(2)}, u32[]{:S(2)}) %collective-permute-start.4) | collective-permute-done | bytes 65568 | tf_op jit(solution)/shard_map/ppermute | solution.py:36
  25.2 0.0 collective-permute-start.6
  25.3 0.0 collective-permute-done.5
  25.3 4.5 %collective-permute-done.6 = bf16[4,8,1024]{2,0,1:T(4,128)(2,1)S(1)} collective-permute-done((bf16[4,8,1024]{2,0,1:T(4,128)(2,1)S(1)}, bf16[4,8,1024]{2,0,1:T(4,128)(2,1)S(1)}, u32[]{:S(2)}, u32[]{:S(2)}) %collective-permute-start.6) | collective-permute-done | bytes 65568 | tf_op jit(solution)/shard_map/ppermute | solution.py:36
  29.9 0.2 fusion.13
  30.1 0.8 slice.17
  30.9 19.0 %psum.42 = f32[32,4]{1,0:T(8,128)S(1)} all-reduce(f32[32,4]{1,0:T(8,128)S(1)} %fusion.13), channel_id=1, replica_groups=mesh['dp'=4,'tensor'=8] {'dp'}, use_global_device_ids=true, to_apply=%region_1.2 | all-reduce | flops 128 | bytes 1024 | tf_op jit(solution)/shard_map/psum | solution.py:49
  49.9 0.2 fusion.15
  50.1 0.1 reshape.35
  50.2 0.0 slice-start
  50.2 1.9 reshape.36
  52.1 5.3 %convolution_convert_fusion.4 = bf16[128,3584]{1,0:T(8,128)(2,1)} fusion(bf16[128,1024]{1,0:T(8,128)(2,1)S(1)} %reshape.35, bf16[1024,3584]{1,0:T(8,128)(2,1)} %param.10), kind=kOutput, calls=%fused_computation.4 | convolution fusion | flops 939982848 | bytes 8519680 | tf_op jit(solution)/shard_map/dot_general | solution.py:58
  57.4 2.1 convolution_convert_fusion.5
  59.5 0.0 slice-done.5
  59.5 3.5 %convolution_convert_fusion.3 = bf16[128,3584]{1,0:T(8,128)(2,1)} fusion(bf16[128,1024]{1,0:T(8,128)(2,1)S(1)} %copy-done, bf16[3584,1024]{1,0:T(8,128)(2,1)S(1)} %bitcast.49), kind=kOutput, calls=%fused_computation.3 | convolution fusion | flops 939982848 | bytes 8519680 | tf_op jit(solution)/shard_map/dot_general | solution.py:59
  63.0 0.0 all-reduce.4.cloned.1.call-update
  63.0 0.2 reduce-scatter.2.cloned.1.call-start
  63.2 0.4 copy-done.13
  63.6 0.1 mul.147
  63.7 0.1 copy.37
  63.8 104.8 %all-reduce.4.cloned.1.call-done = (bf16[128,3584]{1,0:T(8,128)(2,1)}, bf16[128,3584]{1,0:T(8,128)(2,1)}, bf16[128,3584]{1,0:T(8,128)(2,1)}) async-done(((bf16[128,3584]{1,0:T(8,128)(2,1)}, bf16[128,3584]{1,0:T(8,128)(2,1)}, bf16[128,3584]{1,0:T(8,128)(2,1)}), (bf16[128,3584]{1,0:T(8,128)(2,1)}, bf16[128,3584]{1,0:T(8,128)(2,1)}, bf16[128,3584]{1,0:T(8,128)(2,1)})) %all-reduce.4.cloned.1.call-update) | async-done | bytes 2752528 | tf_op jit(solution)/shard_map/psum | solution.py:64
  168.6 5.9 %convolution_convert_fusion.6 = bf16[128,1024]{1,0:T(8,128)(2,1)} fusion(bf16[3584,1024]{1,0:T(8,128)(2,1)} %param.11, bf16[128,3584]{1,0:T(8,128)(2,1)} %get-tuple-element.11, f32[128]{0:T(128)S(1)} %mul.147, bf16[128,3584]{1,0:T(8,128)(2,1)} %get-tuple-element.13), kind=kOutput, calls=%fused_computation.26 | convolution fusion | flops 943783936 | bytes 9437696 | tf_op jit(solution)/shard_map/dot_general | solution.py:71
  174.6 0.0 copy-done.10
  174.6 5.4 %convolution_convert_fusion = bf16[3584,1024]{1,0:T(8,128)(2,1)} fusion(bf16[128,1024]{1,0:T(8,128)(2,1)S(1)} %copy-done.1, bf16[128,3584]{1,0:T(8,128)(2,1)S(1)} %copy-done.6, f32[128]{0:T(128)S(1)} %mul.147, bf16[128,3584]{1,0:T(8,128)(2,1)S(1)} %copy-done.10), kind=kOutput, calls=%fused_computation | convolution fusion | flops 947322880 | bytes 9437696 | tf_op jit(solution)/shard_map/dot_general | solution.py:89
  180.0 1.9 stack_reshape.8
  181.9 1.7 copy.33
  183.7 6.6 %fusion.32 = f32[128,1024]{1,0:T(8,128)S(1)} fusion(bf16[1024,3584]{1,0:T(8,128)(2,1)} %param.9, bf16[128,3584]{1,0:T(8,128)(2,1)} %get-tuple-element.11, bf16[128,3584]{1,0:T(8,128)(2,1)} %get-tuple-element.12, bf16[128,3584]{1,0:T(8,128)(2,1)} %get-tuple-element.13, f32[128]{0:T(128)S(1)} %mul.147), kind=kOutput, calls=%fused_computation.66 | convolution fusion | flops 945946624 | bytes 10617344 | tf_op jit(solution)/shard_map/dot_general | solution.py:72
  190.3 3.3 %fusion.12 = bf16[128,1024]{1,0:T(8,128)(2,1)} fusion(f32[128,1024]{1,0:T(8,128)S(1)} %fusion.32, bf16[1024,3584]{1,0:T(8,128)(2,1)S(1)} %bitcast.47, bf16[128,3584]{1,0:T(8,128)(2,1)S(1)} %copy-done.8, f32[128]{0:T(128)S(1)} %mul.147, bf16[128,3584]{1,0:T(8,128)(2,1)S(1)} %copy-done.11), kind=kOutput, calls=%fused_computation.25 | convolution fusion | flops 943915008 | bytes 9961984 | tf_op jit(solution)/shard_map/dot_general | solution.py:74
  193.6 1.2 stack_reshape.9
  194.8 0.1 copy.34
  194.9 1.0 pad_maximum_fusion
  195.9 1.1 copy.35
  197.0 0.0 reduce-scatter.2.cloned.1.call-update
  197.0 0.0 copy-done.9
  197.0 0.0 copy-done.12
  197.0 0.0 copy-start.7
  197.0 5.4 %convolution_convert_fusion.1 = bf16[1024,3584]{1,0:T(8,128)(2,1)} fusion(bf16[128,1024]{1,0:T(8,128)(2,1)S(1)} %reshape.35, bf16[128,3584]{1,0:T(8,128)(2,1)S(1)} %copy-done.9, f32[128]{0:T(128)S(1)} %mul.147, bf16[128,3584]{1,0:T(8,128)(2,1)S(1)} %copy-done.12), kind=kOutput, calls=%fused_computation.1 | convolution fusion | flops 947322880 | bytes 9437696 | tf_op jit(solution)/shard_map/dot_general | solution.py:95
  202.4 0.0 copy-done.7
  202.4 5.4 %convolution_convert_fusion.2 = bf16[1024,3584]{1,0:T(8,128)(2,1)} fusion(bf16[128,1024]{1,0:T(8,128)(2,1)S(1)} %reshape.35, bf16[128,3584]{1,0:T(8,128)(2,1)S(1)} %copy-done.7, bf16[128,3584]{1,0:T(8,128)(2,1)S(1)} %copy-done.9, bf16[128,3584]{1,0:T(8,128)(2,1)S(1)} %copy-done.12, f32[128]{0:T(128)S(1)} %mul.147), kind=kOutput, calls=%fused_computation.2 | convolution fusion | flops 949616640 | bytes 10355200 | tf_op jit(solution)/shard_map/dot_general | solution.py:92
  207.8 22.5 %reduce-scatter.2.cloned.1.call-done = bf16[4,8,1024]{2,1,0:T(8,128)(2,1)} async-done(((bf16[32,8,1024]{2,1,0:T(8,128)(2,1)}), bf16[4,8,1024]{2,1,0:T(8,128)(2,1)}) %reduce-scatter.2.cloned.1.call-update) | async-done | bytes 65552 | tf_op jit(solution)/shard_map/reduce_scatter | solution.py:83
  230.3 0.9 copy.41
  231.2 0.0 copy-done.2
  231.2 0.1 fusion.21
  231.3 0.1 dynamic_update_slice.41
  231.4 39.5 %all-reduce = (f32[8,4,4]{2,1,0:T(4,128)S(1)}, f32[4,1024]{1,0:T(4,128)S(1)}) all-reduce(f32[8,4,4]{2,1,0:T(4,128)S(1)} %constant_dynamic-update-slice_fusion, f32[4,1024]{1,0:T(4,128)S(1)} %dynamic_update_slice.41), channel_id=1, replica_groups=mesh['dp'=4,'tensor'=8] {'dp','tensor'}, use_global_device_ids=true, to_apply=%region_7.8 | all-reduce | flops 4224 | bytes 33792 | tf_op jit(solution)/shard_map/psum | solution.py:107
  271.0 0.0 copy-start.5
  271.0 0.1 copy.39
  271.1 0.1 copy.40
  271.2 0.7 fusion.19
  271.9 0.6 constant_dynamic-slice_fusion
  (49 shorter events, 0.3 us)
Async XLA Ops:
  7.2 42.7 %copy-start.4 = (f32[1024]{0:T(1024)S(1)}, f32[1024]{0:T(1024)}, u32[]{:S(2)}) copy-start(f32[1024]{0:T(1024)} %param.8) | copy-start | bytes 12292
  7.2 161.5 %all-reduce.4.cloned.1.call-start = ((), (), s32[]{:S(2)}) async-start(), calls=%async_computation.2 | async-start | bytes 5505024 | tf_op jit(solution)/shard_map/psum | solution.py:64
  8.0 5.3 %collective-permute-start.1 = (bf16[4,8,1024]{2,0,1:T(4,128)(2,1)S(1)}, bf16[4,8,1024]{2,0,1:T(4,128)(2,1)S(1)}, u32[]{:S(2)}, u32[]{:S(2)}) collective-permute-start(bf16[4,8,1024]{2,0,1:T(4,128)(2,1)S(1)} %maximum_bitcast_fusion), channel_id=1, source_target_pairs={{0,7},{1,0},{2,1},{3,2},{4,3},{5,4},{6,5},{7,6},{8,15},{9,8},{10,9... | collective-permute-start | bytes 196616 | tf_op jit(solution)/shard_map/ppermute | solution.py:39
  11.5 4.6 %collective-permute-start = (bf16[4,8,1024]{2,0,1:T(4,128)(2,1)S(1)}, bf16[4,8,1024]{2,0,1:T(4,128)(2,1)S(1)}, u32[]{:S(2)}, u32[]{:S(2)}) collective-permute-start(bf16[4,8,1024]{2,0,1:T(4,128)(2,1)S(1)} %maximum_bitcast_fusion), channel_id=1, source_target_pairs={{0,1},{1,2},{2,3},{3,4},{4,5},{5,6},{6,7},{7,0},{8,9},{9,10},{10,1... | collective-permute-start | bytes 196616 | tf_op jit(solution)/shard_map/ppermute | solution.py:36
  13.4 4.6 %collective-permute-start.3 = (bf16[4,8,1024]{2,0,1:T(4,128)(2,1)S(1)}, bf16[4,8,1024]{2,0,1:T(4,128)(2,1)S(1)}, u32[]{:S(2)}, u32[]{:S(2)}) collective-permute-start(bf16[4,8,1024]{2,0,1:T(4,128)(2,1)S(1)} %collective-permute-done.1), channel_id=1, source_target_pairs={{0,7},{1,0},{2,1},{3,2},{4,3},{5,4},{6,5},{7,6},{8,15},{9,8},{10,9... | collective-permute-start | bytes 196616 | tf_op jit(solution)/shard_map/ppermute | solution.py:39
  16.1 4.6 %collective-permute-start.2 = (bf16[4,8,1024]{2,0,1:T(4,128)(2,1)S(1)}, bf16[4,8,1024]{2,0,1:T(4,128)(2,1)S(1)}, u32[]{:S(2)}, u32[]{:S(2)}) collective-permute-start(bf16[4,8,1024]{2,0,1:T(4,128)(2,1)S(1)} %collective-permute-done), channel_id=1, source_target_pairs={{0,1},{1,2},{2,3},{3,4},{4,5},{5,6},{6,7},{7,0},{8,9},{9,10},{10,1... | collective-permute-start | bytes 196616 | tf_op jit(solution)/shard_map/ppermute | solution.py:36
  18.0 7.3 %collective-permute-start.5 = (bf16[4,8,1024]{2,0,1:T(4,128)(2,1)S(1)}, bf16[4,8,1024]{2,0,1:T(4,128)(2,1)S(1)}, u32[]{:S(2)}, u32[]{:S(2)}) collective-permute-start(bf16[4,8,1024]{2,0,1:T(4,128)(2,1)S(1)} %collective-permute-done.3), channel_id=1, source_target_pairs={{0,7},{1,0},{2,1},{3,2},{4,3},{5,4},{6,5},{7,6},{8,15},{9,8},{10,9... | collective-permute-start | bytes 196616 | tf_op jit(solution)/shard_map/ppermute | solution.py:39
  20.6 4.6 %collective-permute-start.4 = (bf16[4,8,1024]{2,0,1:T(4,128)(2,1)S(1)}, bf16[4,8,1024]{2,0,1:T(4,128)(2,1)S(1)}, u32[]{:S(2)}, u32[]{:S(2)}) collective-permute-start(bf16[4,8,1024]{2,0,1:T(4,128)(2,1)S(1)} %collective-permute-done.2), channel_id=1, source_target_pairs={{0,1},{1,2},{2,3},{3,4},{4,5},{5,6},{6,7},{7,0},{8,9},{9,10},{10,1... | collective-permute-start | bytes 196616 | tf_op jit(solution)/shard_map/ppermute | solution.py:36
  25.2 4.6 %collective-permute-start.6 = (bf16[4,8,1024]{2,0,1:T(4,128)(2,1)S(1)}, bf16[4,8,1024]{2,0,1:T(4,128)(2,1)S(1)}, u32[]{:S(2)}, u32[]{:S(2)}) collective-permute-start(bf16[4,8,1024]{2,0,1:T(4,128)(2,1)S(1)} %collective-permute-done.4), channel_id=1, source_target_pairs={{0,1},{1,2},{2,3},{3,4},{4,5},{5,6},{6,7},{7,0},{8,9},{9,10},{10,1... | collective-permute-start | bytes 196616 | tf_op jit(solution)/shard_map/ppermute | solution.py:36
  50.2 7.2 %slice-start = ((s8[7340032]{0:T(1024)(128)(4,1)}), s8[3145728]{0:T(1024)(128)(4,1)S(1)}, s32[]{:S(2)}) async-start(s8[7340032]{0:T(1024)(128)(4,1)} %bitcast.44), calls=%async_computation.3 | async-start | bytes 6291456
  52.1 5.3 %slice-start.1 = ((s8[7340032]{0:T(1024)(128)(4,1)}), s8[4194304]{0:T(1024)(128)(4,1)S(1)}, s32[]{:S(2)}) async-start(s8[7340032]{0:T(1024)(128)(4,1)} %bitcast.44), calls=%async_computation.4 | async-start | bytes 8388608
  52.1 7.4 %slice-start.4 = ((s8[7340032]{0:T(1024)(128)(4,1)}), s8[4194304]{0:T(1024)(128)(4,1)S(1)}, s32[]{:S(2)}) async-start(s8[7340032]{0:T(1024)(128)(4,1)} %bitcast.48), calls=%async_computation.7 | async-start | bytes 8388608
  57.4 2.1 slice-start.5
  57.4 2.1 copy-start
  62.9 0.7 copy-start.13
  63.0 167.3 %reduce-scatter.2.cloned.1.call-start = ((), (), s32[]{:S(2)}) async-start(), calls=%async_computation.1 | async-start | bytes 589824 | tf_op jit(solution)/shard_map/reduce_scatter | solution.py:83
  168.6 5.9 %copy-start.1 = (bf16[128,1024]{1,0:T(8,128)(2,1)S(1)}, bf16[128,1024]{1,0:T(8,128)(2,1)}, u32[]{:S(2)}) copy-start(bf16[128,1024]{1,0:T(8,128)(2,1)} %reshape.36) | copy-start | bytes 786436
  168.6 5.9 %copy-start.6 = (bf16[128,3584]{1,0:T(8,128)(2,1)S(1)}, bf16[128,3584]{1,0:T(8,128)(2,1)}, u32[]{:S(2)}) copy-start(bf16[128,3584]{1,0:T(8,128)(2,1)} %get-tuple-element.11) | copy-start | bytes 2752516
  168.6 5.9 %copy-start.10 = (bf16[128,3584]{1,0:T(8,128)(2,1)S(1)}, bf16[128,3584]{1,0:T(8,128)(2,1)}, u32[]{:S(2)}) copy-start(bf16[128,3584]{1,0:T(8,128)(2,1)} %get-tuple-element.13) | copy-start | bytes 2752516
  180.0 10.3 %slice-start.2 = ((s8[7340032]{0:T(1024)(128)(4,1)}), s8[3145728]{0:T(1024)(128)(4,1)S(1)}, s32[]{:S(2)}) async-start(s8[7340032]{0:T(1024)(128)(4,1)} %bitcast.46), calls=%async_computation.5 | async-start | bytes 6291456
  183.6 6.6 %slice-start.3 = ((s8[7340032]{0:T(1024)(128)(4,1)}), s8[4194304]{0:T(1024)(128)(4,1)S(1)}, s32[]{:S(2)}) async-start(s8[7340032]{0:T(1024)(128)(4,1)} %bitcast.46), calls=%async_computation.6 | async-start | bytes 8388608
  183.7 6.6 %copy-start.8 = (bf16[128,3584]{1,0:T(8,128)(2,1)S(1)}, bf16[128,3584]{1,0:T(8,128)(2,1)}, u32[]{:S(2)}) copy-start(bf16[128,3584]{1,0:T(8,128)(2,1)} %get-tuple-element.12) | copy-start | bytes 2752516
  183.7 6.6 %copy-start.11 = (bf16[128,3584]{1,0:T(8,128)(2,1)S(1)}, bf16[128,3584]{1,0:T(8,128)(2,1)}, u32[]{:S(2)}) copy-start(bf16[128,3584]{1,0:T(8,128)(2,1)} %get-tuple-element.13) | copy-start | bytes 2752516
  193.6 3.4 %copy-start.9 = (bf16[128,3584]{1,0:T(8,128)(2,1)S(1)}, bf16[128,3584]{1,0:T(8,128)(2,1)}, u32[]{:S(2)}) copy-start(bf16[128,3584]{1,0:T(8,128)(2,1)} %get-tuple-element.12) | copy-start | bytes 2752516
  193.6 3.4 %copy-start.12 = (bf16[128,3584]{1,0:T(8,128)(2,1)S(1)}, bf16[128,3584]{1,0:T(8,128)(2,1)}, u32[]{:S(2)}) copy-start(bf16[128,3584]{1,0:T(8,128)(2,1)} %get-tuple-element.13) | copy-start | bytes 2752516
  197.0 5.4 %copy-start.7 = (bf16[128,3584]{1,0:T(8,128)(2,1)S(1)}, bf16[128,3584]{1,0:T(8,128)(2,1)}, u32[]{:S(2)}) copy-start(bf16[128,3584]{1,0:T(8,128)(2,1)} %get-tuple-element.11) | copy-start | bytes 2752516
  202.4 28.8 %copy-start.2 = (bf16[4,4,1024]{2,1,0:T(4,128)(2,1)S(1)}, bf16[4,4,1024]{2,1,0:T(4,128)(2,1)}, u32[]{:S(2)}) copy-start(bf16[4,4,1024]{2,1,0:T(4,128)(2,1)} %param.7) | copy-start | bytes 98308
  202.4 68.8 %copy-start.3 = (bf16[4,4,1024]{2,1,0:T(4,128)(2,1)S(1)}, bf16[4,4,1024]{2,1,0:T(4,128)(2,1)}, u32[]{:S(2)}) copy-start(bf16[4,4,1024]{2,1,0:T(4,128)(2,1)} %param.12) | copy-start | bytes 98308
  271.0 1.5 copy-start.5
Sparse Core Ops, SparseCore 0:
  63.1 105.4 all-reduce.3
  197.1 33.1 reduce-scatter.1
